TPU v7x, 32 devices: a whole 2x2x4 slice. The times are simulated.
32 devices in a mesh: row: 8 (over z, core), col: 4 (over y, x).
Axes of the slice: x: 2, y: 2, z: 4, core: 2. Of those that a mesh axis runs over, the one named last changes fastest.
Arguments:
- trunk_in: bfloat16 [1536, 8192], P('col', 'row'), may hold values from -24 to 24
- conv_weight: bfloat16 [5, 1536, 1536], P(None, 'col'), may hold values from -0.0625 to 0.0625
- conv_bias: float32 [1536], P('col'), may hold values from -3 to 3
- norm_gain: float32 [1536], replicated, may hold values from 0.1 to 1.9
- pair_proj: bfloat16 [64, 1536], replicated, may hold values from -0.15625 to 0.15625
- pair_in: bfloat16 [512, 128, 128], P('row', 'col'), may hold values from -6 to 6
- opm_weight: bfloat16 [1024, 128], replicated, may hold values from -0.1875 to 0.1875
- pair_bias: float32 [128], replicated, may hold values from -3 to 3
Outputs:
- trunk_out: bfloat16 [1536, 8192], P('col', 'row')
- pair_out: bfloat16 [512, 128, 128], P('row', 'col')
All inputs are finite; a program needn't handle non-finite values.
Results may differ from a plain program's by a relative error of at most 0.012.
Values may be sent and summed in bfloat16 or wider, within the bound.
No kernel may reach another device: no remote copies, remote signals or barrier semaphores. Data moves between devices by JAX's collectives and lax.ppermute only.
A program may use at most 64 MiB of HBM per device.

v0:
```python
import jax
import jax.numpy as jnp
from jax import lax
from jax.sharding import PartitionSpec as P

TRUNK_CHANNELS = 1536
DILATION_STEP = 8
POOL = 16
OPM = 32
WINDOWS = 4
EPSILON = 1e-05


def with_halo(cells, sides, width):
    for axis, dim in sides:
        count = lax.axis_size(axis)
        ends = count - 1
        head = lax.slice_in_dim(cells, 0, width, axis=dim)
        tail = lax.slice_in_dim(cells, cells.shape[dim] - width, cells.shape[dim], axis=dim)
        cells = jnp.concatenate(
            [
                lax.ppermute(tail, axis, [(i, (i + 1) % count) for i in range(ends)]),
                cells,
                lax.ppermute(head, axis, [((i + 1) % count, i) for i in range(ends)]),
            ],
            axis=dim,
        )
    return cells


def partner_2(block, axis, bit):
    count = lax.axis_size(axis)
    route = []
    for low in range(count):
        high = low | 1 << bit
        if high != low and high < count:
            route += [(low, high), (high, low)]
    return lax.ppermute(block, axis, route)


def per_device(
    trunk_in, conv_weight, conv_bias, norm_gain, pair_proj, pair_in, opm_weight, pair_bias
):
    local_channels = trunk_in.shape[0]
    token_positions = trunk_in.shape[1]
    kernel = conv_weight.shape[0]
    border_width = 2 * DILATION_STEP
    per_window = lax.axis_size("row") // WINDOWS
    row_index = lax.axis_index("row")
    col_index = lax.axis_index("col")
    in_window = row_index % per_window
    source = trunk_in.astype(jnp.float32)
    zero_sum = jnp.zeros((local_channels, token_positions), jnp.float32)
    squares = lax.psum(jnp.sum(source * source, axis=0), "col")
    scale = lax.rsqrt(squares / TRUNK_CHANNELS + EPSILON)[None, :]
    own_gain = lax.dynamic_slice_in_dim(norm_gain, col_index * local_channels, local_channels, 0)
    gelu_output = jax.nn.gelu(source * own_gain[:, None] * scale).astype(jnp.bfloat16)
    padded_trunk = with_halo(gelu_output, (("row", 1),), border_width)
    carried = zero_sum
    piece = lax.all_gather(padded_trunk, "col", axis=0, tiled=True)
    for tap_offset in range(kernel):
        carried = carried + jnp.dot(
            conv_weight[tap_offset],
            piece[:, tap_offset * DILATION_STEP : tap_offset * DILATION_STEP + token_positions],
            preferred_element_type=jnp.float32,
        )
    trunk_out = (source + carried + conv_bias[:, None]).astype(jnp.bfloat16)
    pooled = (
        trunk_out.astype(jnp.float32)
        .reshape(local_channels, token_positions // POOL, POOL)
        .mean(axis=2)
        .astype(jnp.bfloat16)
    )
    own_proj = lax.dynamic_slice_in_dim(pair_proj, col_index * local_channels, local_channels, 1)
    pooled_f = pooled.astype(jnp.float32)
    partial_proj = lax.dot_general(
        pooled, own_proj, (((0,), (1,)), ((), ())), preferred_element_type=jnp.float32
    )
    projected, sums = lax.psum((partial_proj, jnp.sum(pooled_f * pooled_f, axis=0)), "col")
    sides = (projected * lax.rsqrt(sums / TRUNK_CHANNELS + EPSILON)[:, None]).astype(jnp.bfloat16)
    row_side = sides[:, :OPM]
    collected = sides[:, OPM:]
    col_block = pair_in.shape[1]
    pooled_rows = row_side.shape[0]
    for bit_num in range(per_window.bit_length() - 1):
        partner = partner_2(collected, "row", bit_num)
        upper_half = in_window // 2**bit_num % 2 == 1
        collected = jnp.where(
            upper_half,
            jnp.concatenate([partner, collected], axis=0),
            jnp.concatenate([collected, partner], axis=0),
        )
    own_cols = lax.dynamic_slice_in_dim(collected, col_index * col_block, col_block, 0)
    outer = (
        row_side.astype(jnp.float32)[:, None, :, None]
        * own_cols.astype(jnp.float32)[None, :, None, :]
    ).astype(jnp.bfloat16)
    outer = outer.reshape(pooled_rows * col_block, OPM * OPM)
    update = jnp.dot(outer, opm_weight, preferred_element_type=jnp.float32).reshape(pair_in.shape)
    pair_out = (pair_in.astype(jnp.float32) + update + pair_bias).astype(jnp.bfloat16)
    return (trunk_out, pair_out)


def solution(mesh):
    return jax.shard_map(
        per_device,
        mesh=mesh,
        in_specs=(
            P("col", "row"),
            P(None, "col", None),
            P("col"),
            P(),
            P(),
            P("row", "col", None),
            P(),
            P(),
        ),
        out_specs=(P("col", "row"), P("row", "col", None)),
        check_vma=False,
    )
```

profile of v0, /device:TPU:0, one launch (start us, length us, event | category | flops | bytes accessed | tf_op | source)
XLA Modules:
  0.0 115.7 jit_solution(4807338806114271744)
XLA Ops:
  7.2 0.0 copy-start
  7.2 0.0 all-gather.2.cloned.1.call-start
  7.2 1.5 %copy.25 = bf16[384,1024]{0,1:T(8,128)(2,1)S(1)} copy(bf16[384,1024]{1,0:T(8,128)(2,1)} %param.8) | data formatting | bytes 1572864 | tf_op args[0]
  8.8 0.2 fusion.21
  9.0 11.4 %psum.21 = f32[1024]{0:T(1024)S(1)} all-reduce(f32[1024]{0:T(1024)S(1)} %fusion.21), channel_id=1, replica_groups=mesh['row'=8,'col'=4] {'col'}, use_global_device_ids=true, to_apply=%region_1.2 | all-reduce | flops 1024 | bytes 8192 | tf_op jit(solution)/shard_map/psum | solution.py:54
  20.4 0.8 dynamic_slice.9
  21.2 0.7 fusion.16
  21.9 1.3 %collective-permute-start = (bf16[384,16]{0,1:T(8,128)(2,1)S(1)}, bf16[384,16]{0,1:T(8,128)(2,1)S(1)}, u32[]{:S(2)}, u32[]{:S(2)}) collective-permute-start(bf16[384,16]{0,1:T(8,128)(2,1)S(1)} %get-tuple-element.12), channel_id=1, source_target_pairs={{0,4},{4,8},{8,12},{12,16},{16,20},{20,24},{24,28},{1,5},{5,9},{9,... | collective-permute-start | bytes 36872 | tf_op jit(solution)/shard_map/ppermute | solution.py:22
  23.2 1.3 %collective-permute-start.1 = (bf16[384,16]{0,1:T(8,128)(2,1)S(1)}, bf16[384,16]{0,1:T(8,128)(2,1)S(1)}, u32[]{:S(2)}, u32[]{:S(2)}) collective-permute-start(bf16[384,16]{0,1:T(8,128)(2,1)S(1)} %get-tuple-element.13), channel_id=1, source_target_pairs={{4,0},{8,4},{12,8},{16,12},{20,16},{24,20},{28,24},{5,1},{9,5},{13... | collective-permute-start | bytes 36872 | tf_op jit(solution)/shard_map/ppermute | solution.py:24
  24.5 3.6 %collective-permute-done.1 = bf16[384,16]{0,1:T(8,128)(2,1)S(1)} collective-permute-done((bf16[384,16]{0,1:T(8,128)(2,1)S(1)}, bf16[384,16]{0,1:T(8,128)(2,1)S(1)}, u32[]{:S(2)}, u32[]{:S(2)}) %collective-permute-start.1) | collective-permute-done | bytes 12320 | tf_op jit(solution)/shard_map/ppermute | solution.py:24
  28.1 1.0 pad_maximum_fusion
  29.1 0.0 all-gather.2.cloned.1.call-update
  29.1 45.1 %all-gather.2.cloned.1.call-done = bf16[1536,1056]{0,1:T(8,128)(2,1)} async-done(((bf16[384,1056]{0,1:T(8,128)(2,1)}), bf16[1536,1056]{0,1:T(8,128)(2,1)}) %all-gather.2.cloned.1.call-update) | async-done | bytes 3244048 | tf_op jit(solution)/shard_map/all_gather | solution.py:60
  74.2 4.2 %fusion.5 = f32[1024,384]{1,0:T(8,128)S(1)} fusion(bf16[1536,1056]{0,1:T(8,128)(2,1)} %all-gather.2.cloned.1.call-done, bf16[5,384,1536]{2,1,0:T(8,128)(2,1)} %param.9), kind=kOutput, calls=%fused_computation.6 | convolution fusion | flops 1207959552 | bytes 5898240 | tf_op jit(solution)/shard_map/dot_general | solution.py:62
  78.4 0.0 slice-start.1
  78.4 3.2 %fusion.7 = f32[1024,384]{1,0:T(8,128)S(1)} fusion(bf16[1536,1056]{0,1:T(8,128)(2,1)S(1)} %copy-done.1, bf16[5,384,1536]{2,1,0:T(8,128)(2,1)} %param.9), kind=kOutput, calls=%fused_computation.8 | convolution fusion | flops 1207959552 | bytes 5898240 | tf_op jit(solution)/shard_map/dot_general | solution.py:62
  81.6 1.8 %fusion.9 = f32[1024,384]{1,0:T(8,128)S(1)} fusion(bf16[1536,1056]{0,1:T(8,128)(2,1)S(1)} %copy-done.1, bf16[5,384,1536]{2,1,0:T(8,128)(2,1)S(1)} %bitcast.28), kind=kOutput, calls=%fused_computation.10 | convolution fusion | flops 1207959552 | bytes 5898240 | tf_op jit(solution)/shard_map/dot_general | solution.py:62
  83.4 0.0 copy-start.3
  83.5 1.8 %fusion.11 = f32[1024,384]{1,0:T(8,128)S(1)} fusion(bf16[1536,1056]{0,1:T(8,128)(2,1)S(1)} %copy-done.1, bf16[5,384,1536]{2,1,0:T(8,128)(2,1)S(1)} %bitcast.28), kind=kOutput, calls=%fused_computation.12 | convolution fusion | flops 1207959552 | bytes 5898240 | tf_op jit(solution)/shard_map/dot_general | solution.py:62
  85.3 2.2 %convert_reduce_fusion = (f32[384,64]{0,1:T(8,128)S(1)}, bf16[384,1024]{0,1:T(8,128)(2,1)S(1)}) fusion(f32[384]{0:T(512)S(1)} %copy-done.3, bf16[5,384,1536]{2,1,0:T(8,128)(2,1)S(1)} %bitcast.28, bf16[1536,1056]{0,1:T(8,128)(2,1)S(1)} %copy-done.1, f32[1024,384]{1,0:T(8,128)S(1)} %fusion.5, f32[1024,384]{1,0:T(8,128)S(1)} %fusion.7, ...), kind=kOutput, calls=%fused_computation.30 | convolution fusion | flops 1211867136 | bytes 12290048 | tf_op jit(solution)/shard_map/dot_general | solution.py:62
  87.5 0.1 multiply_reduce_fusion
  87.6 0.9 fusion.41
  88.6 15.8 %all-reduce = (f32[64,64]{0,1:T(8,128)S(1)}, f32[64]{0:T(128)S(1)}) all-reduce(f32[64,64]{0,1:T(8,128)S(1)} %fusion.41, f32[64]{0:T(128)S(1)} %multiply_reduce_fusion), channel_id=1, replica_groups=mesh['row'=8,'col'=4] {'col'}, use_global_device_ids=true, to_apply=%region_3.4 | all-reduce | flops 4160 | bytes 33280 | tf_op jit(solution)/shard_map/psum | solution.py:79
  104.4 0.1 collective-permute-start.2
  104.5 1.2 %copy.29 = bf16[384,1024]{1,0:T(8,128)(2,1)} copy(bf16[384,1024]{0,1:T(8,128)(2,1)S(1)} %get-tuple-element.17) | data formatting | bytes 1572864
  105.8 0.2 copy.27
  105.9 0.0 collective-permute-done.2
  106.0 0.1 fusion.44
  106.1 0.1 copy.28
  106.2 0.2 mul.102
  106.4 0.3 copy-done.2
  106.8 2.1 %fusion.29 = bf16[64,32,128]{2,1,0:T(8,128)(2,1)} fusion(f32[32,1024]{1,0:T(8,128)S(1)} %mul.102, f32[64,1024]{1,0:T(8,128)S(1)} %copy.27, bf16[64,32,128]{2,1,0:T(8,128)(2,1)S(1)} %copy-done.2, f32[128]{0:T(128)S(1)} %copy-done.4, bf16[1024,128]{1,0:T(8,128)(2,1)S(1)} %copy-done), kind=kOutput, calls=%fused_computation.33 | convolution fusion | flops 542113792 | bytes 1704448 | tf_op jit(solution)/shard_map/dot_general | solution.py:99
  (19 shorter events, 0.1 us)
Async XLA Ops:
  7.2 99.3 %copy-start = (bf16[1024,128]{1,0:T(8,128)(2,1)S(1)}, bf16[1024,128]{1,0:T(8,128)(2,1)}, u32[]{:S(2)}) copy-start(bf16[1024,128]{1,0:T(8,128)(2,1)} %param.14) | copy-start | bytes 786436
  7.2 67.0 %all-gather.2.cloned.1.call-start = ((), (), s32[]{:S(2)}) async-start(), calls=%async_computation | async-start | bytes 4055040 | tf_op jit(solution)/shard_map/all_gather | solution.py:60
  21.9 2.6 %collective-permute-start = (bf16[384,16]{0,1:T(8,128)(2,1)S(1)}, bf16[384,16]{0,1:T(8,128)(2,1)S(1)}, u32[]{:S(2)}, u32[]{:S(2)}) collective-permute-start(bf16[384,16]{0,1:T(8,128)(2,1)S(1)} %get-tuple-element.12), channel_id=1, source_target_pairs={{0,4},{4,8},{8,12},{12,16},{16,20},{20,24},{24,28},{1,5},{5,9},{9,... | collective-permute-start | bytes 36872 | tf_op jit(solution)/shard_map/ppermute | solution.py:22
  23.2 4.9 %collective-permute-start.1 = (bf16[384,16]{0,1:T(8,128)(2,1)S(1)}, bf16[384,16]{0,1:T(8,128)(2,1)S(1)}, u32[]{:S(2)}, u32[]{:S(2)}) collective-permute-start(bf16[384,16]{0,1:T(8,128)(2,1)S(1)} %get-tuple-element.13), channel_id=1, source_target_pairs={{4,0},{8,4},{12,8},{16,12},{20,16},{24,20},{28,24},{5,1},{9,5},{13... | collective-permute-start | bytes 36872 | tf_op jit(solution)/shard_map/ppermute | solution.py:24
  74.2 4.2 %copy-start.1 = (bf16[1536,1056]{0,1:T(8,128)(2,1)S(1)}, bf16[1536,1056]{0,1:T(8,128)(2,1)}, u32[]{:S(2)}) copy-start(bf16[1536,1056]{0,1:T(8,128)(2,1)} %all-gather.2.cloned.1.call-done) | copy-start | bytes 9732100
  74.2 7.4 %slice-start = ((s8[5898240]{0:T(1024)(128)(4,1)}), s8[4194304]{0:T(1024)(128)(4,1)S(1)}, s32[]{:S(2)}) async-start(s8[5898240]{0:T(1024)(128)(4,1)} %bitcast.27), calls=%async_computation.1 | async-start | bytes 8388608
  78.4 3.2 %slice-start.1 = ((s8[5898240]{0:T(1024)(128)(4,1)}), s8[1703936]{0:T(1024)(128)(4,1)S(1)}, s32[]{:S(2)}) async-start(s8[5898240]{0:T(1024)(128)(4,1)} %bitcast.27), calls=%async_computation.2 | async-start | bytes 3407872
  83.4 1.8 %copy-start.3 = (f32[384]{0:T(512)S(1)}, f32[384]{0:T(512)}, u32[]{:S(2)}) copy-start(f32[384]{0:T(512)} %param.10) | copy-start | bytes 4612
  104.4 1.5 %collective-permute-start.2 = (bf16[64,32]{0,1:T(8,128)(2,1)S(1)}, bf16[64,32]{0,1:T(8,128)(2,1)S(1)}, u32[]{:S(2)}, u32[]{:S(2)}) collective-permute-start(bf16[64,32]{0,1:T(8,128)(2,1)S(1)} %get-tuple-element.15), channel_id=1, source_target_pairs={{0,4},{4,0},{8,12},{12,8},{16,20},{20,16},{24,28},{28,24},{1,5},{5... | collective-permute-start | bytes 12296 | tf_op jit(solution)/shard_map/ppermute | solution.py:38
  105.7 1.0 copy-start.2
  105.7 1.0 copy-start.4
Sparse Core Ops, SparseCore 0:
  29.2 44.9 all-gather.1
where the time goes:
time: 116 us
  waiting for transfers between devices  48.7 us (42%)
  blocking collectives  27.2 us (23%)
  matrix products  16.2 us (14%)
  between operations  14.3 us (12%)
  local copies, waits for them, and re-layouts  4.39 us (4%)
  starting transfers between devices  2.69 us (2%)
  other arithmetic  2.16 us (2%)
    all_gather x1, waiting for transfers between devices, per_device(): piece = lax.all_gather(padded_trunk, 'col', axis=0, tiled=True)  45.1 us
    psum x1, blocking collectives, per_device(): lax.psum((partial_proj, jnp.sum(pooled_f * pooled_f, axis=0)), 'col')  15.8 us
    dot_general x5, matrix products, per_device(): jnp.dot(conv_weight[tap_offset], piece[:, tap_offset * DILATION_STEP:tap_...  13.2 us
    psum x1, blocking collectives, per_device(): squares = lax.psum(jnp.sum(source * source, axis=0), 'col')  11.4 us
    ppermute x1, waiting for transfers between devices, with_halo(): lax.ppermute(head, axis, [((i + 1) % count, i) for i in range(ends)])  3.57 us
    unnamed x16, local copies, waits for them, and re-layouts  3.06 us
  transfers between devices with their start and end apart: 4, of which 2 were waited for; matrix products, arithmetic and copies ran while one was open for 1% of the time, Pallas kernels for 0%

commit v1 on v0

--- a/solution.py
+++ b/solution.py
@@ -57,7 +57,9 @@
     gelu_output = jax.nn.gelu(source * own_gain[:, None] * scale).astype(jnp.bfloat16)
     padded_trunk = with_halo(gelu_output, (("row", 1),), border_width)
     carried = zero_sum
-    piece = lax.all_gather(padded_trunk, "col", axis=0, tiled=True)
+    piece = jnp.concatenate(
+        lax.all_to_all(jnp.stack([padded_trunk] * lax.axis_size("col")), "col", 0, 0), axis=0
+    )
     for tap_offset in range(kernel):
         carried = carried + jnp.dot(
             conv_weight[tap_offset],

time: 116 us -> 93.9 us (0.81)
  waiting for transfers between devices: 48.7 us -> 3.58 us
  blocking collectives: 27.2 us -> 66.9 us
  between operations: 14.3 us -> 0.89 us
  matrix products: 16.2 us -> 12.4 us
    all_gather x1 -> x0, waiting for transfers between devices: 45.1 us -> none  [per_device(): piece = lax.all_gather(padded_trunk, 'col', axis=0, tiled=True)]
    all_to_all x0 -> x1, blocking collectives: none -> 40.3 us  [per_device(): lax.all_to_all(jnp.stack([padded_trunk] * lax.axis_size('col')), 'col', 0...]
    dot_general x5, matrix products: 13.2 us -> 9.43 us  [per_device(): jnp.dot(conv_weight[tap_offset], piece[:, tap_offset * DILATION_STEP:tap_...]
    unnamed x16 -> x14, local copies, waits for them, and re-layouts: 3.06 us -> 3.06 us
  transfers between devices with their start and end apart: 4 -> 3, of which waited for: 2 -> 1; matrix products, arithmetic and copies ran while one was open for 1% -> 1% of each run, Pallas kernels for 0% -> 0%
where the time goes in v1:
time: 93.9 us; the launch traced here: 92.8 us
  blocking collectives  66.9 us (71%)
  matrix products  12.4 us (13%)
  local copies, waits for them, and re-layouts  5.03 us (5%)
  waiting for transfers between devices  3.58 us (4%)
  starting transfers between devices  2.65 us (3%)
  other arithmetic  1.25 us (1%)
    all_to_all x1, blocking collectives, per_device(): lax.all_to_all(jnp.stack([padded_trunk] * lax.axis_size('col')), 'col', 0...  40.3 us
    psum x1, blocking collectives, per_device(): lax.psum((partial_proj, jnp.sum(pooled_f * pooled_f, axis=0)), 'col')  15.2 us
    psum x1, blocking collectives, per_device(): squares = lax.psum(jnp.sum(source * source, axis=0), 'col')  11.4 us
    dot_general x5, matrix products, per_device(): jnp.dot(conv_weight[tap_offset], piece[:, tap_offset * DILATION_STEP:tap_...  9.43 us
    ppermute x1, waiting for transfers between devices, with_halo(): lax.ppermute(head, axis, [((i + 1) % count, i) for i in range(ends)])  3.57 us
    unnamed x14, local copies, waits for them, and re-layouts  3.06 us
    dot_general x1, matrix products, per_device(): jnp.dot(outer, opm_weight, preferred_element_type=jnp.float32)  2.05 us
  transfers between devices with their start and end apart: 3, of which 1 were waited for; matrix products, arithmetic and copies ran while one was open for 1% of the time, Pallas kernels for 0%

profile of v1, /device:TPU:0, one launch (start us, length us, event | category | flops | bytes accessed | tf_op | source)
XLA Modules:
  0.0 92.8 jit_solution(13858245376016779937)
XLA Ops:
  0.6 0.0 copy-start
  0.7 1.5 %copy.37 = bf16[384,1024]{0,1:T(8,128)(2,1)S(1)} copy(bf16[384,1024]{1,0:T(8,128)(2,1)} %param.8) | data formatting | bytes 1572864 | tf_op args[0]
  2.2 0.2 fusion.21
  2.4 11.4 %psum.21 = f32[1024]{0:T(1024)S(1)} all-reduce(f32[1024]{0:T(1024)S(1)} %fusion.21), channel_id=1, replica_groups=mesh['row'=8,'col'=4] {'col'}, use_global_device_ids=true, to_apply=%region_1.2 | all-reduce | flops 1024 | bytes 8192 | tf_op jit(solution)/shard_map/psum | solution.py:54
  13.8 0.8 dynamic_slice.9
  14.6 0.7 fusion.16
  15.3 1.3 %collective-permute-start = (bf16[384,16]{0,1:T(8,128)(2,1)S(1)}, bf16[384,16]{0,1:T(8,128)(2,1)S(1)}, u32[]{:S(2)}, u32[]{:S(2)}) collective-permute-start(bf16[384,16]{0,1:T(8,128)(2,1)S(1)} %get-tuple-element.14), channel_id=1, source_target_pairs={{0,4},{4,8},{8,12},{12,16},{16,20},{20,24},{24,28},{1,5},{5,9},{9,... | collective-permute-start | bytes 36872 | tf_op jit(solution)/shard_map/ppermute | solution.py:22
  16.6 1.3 %collective-permute-start.1 = (bf16[384,16]{0,1:T(8,128)(2,1)S(1)}, bf16[384,16]{0,1:T(8,128)(2,1)S(1)}, u32[]{:S(2)}, u32[]{:S(2)}) collective-permute-start(bf16[384,16]{0,1:T(8,128)(2,1)S(1)} %get-tuple-element.15), channel_id=1, source_target_pairs={{4,0},{8,4},{12,8},{16,12},{20,16},{24,20},{28,24},{5,1},{9,5},{13... | collective-permute-start | bytes 36872 | tf_op jit(solution)/shard_map/ppermute | solution.py:24
  17.9 3.6 %collective-permute-done.1 = bf16[384,16]{0,1:T(8,128)(2,1)S(1)} collective-permute-done((bf16[384,16]{0,1:T(8,128)(2,1)S(1)}, bf16[384,16]{0,1:T(8,128)(2,1)S(1)}, u32[]{:S(2)}, u32[]{:S(2)}) %collective-permute-start.1) | collective-permute-done | bytes 12320 | tf_op jit(solution)/shard_map/ppermute | solution.py:24
  21.5 0.1 pad_maximum_fusion
  21.6 0.0 slice-start
  21.6 0.3 stack.2
  21.9 0.0 slice-start.1
  21.9 40.3 %all_to_all.5 = bf16[4,384,1056]{1,2,0:T(8,128)(2,1)S(1)} all-to-all(bf16[4,384,1056]{1,2,0:T(8,128)(2,1)S(1)} %stack.2), channel_id=1, replica_groups=mesh['row'=8,'col'=4] {'col'}, dimensions={0} | all-to-all | bytes 6488064 | tf_op jit(solution)/shard_map/all_to_all | solution.py:61
  62.2 0.3 copy.44
  62.6 1.8 %fusion.3 = f32[1024,384]{1,0:T(8,128)S(1)} fusion(bf16[1536,1056]{0,1:T(8,128)(2,1)S(1)} %bitcast.29, bf16[5,384,1536]{2,1,0:T(8,128)(2,1)S(1)} %bitcast.36), kind=kOutput, calls=%fused_computation.4 | convolution fusion | flops 1207959552 | bytes 5898240 | tf_op jit(solution)/shard_map/dot_general | solution.py:64
  64.4 1.8 %fusion.5 = f32[1024,384]{1,0:T(8,128)S(1)} fusion(bf16[1536,1056]{0,1:T(8,128)(2,1)S(1)} %bitcast.30, bf16[5,384,1536]{2,1,0:T(8,128)(2,1)S(1)} %bitcast.36), kind=kOutput, calls=%fused_computation.6 | convolution fusion | flops 1207959552 | bytes 5898240 | tf_op jit(solution)/shard_map/dot_general | solution.py:64
  66.2 1.8 %fusion.7 = f32[1024,384]{1,0:T(8,128)S(1)} fusion(bf16[1536,1056]{0,1:T(8,128)(2,1)S(1)} %bitcast.31, bf16[5,384,1536]{2,1,0:T(8,128)(2,1)S(1)} %bitcast.36), kind=kOutput, calls=%fused_computation.8 | convolution fusion | flops 1207959552 | bytes 5898240 | tf_op jit(solution)/shard_map/dot_general | solution.py:64
  68.0 0.0 copy-start.2
  68.0 1.8 %fusion.9 = f32[1024,384]{1,0:T(8,128)S(1)} fusion(bf16[1536,1056]{0,1:T(8,128)(2,1)S(1)} %bitcast.32, bf16[5,384,1536]{2,1,0:T(8,128)(2,1)S(1)} %bitcast.36), kind=kOutput, calls=%fused_computation.10 | convolution fusion | flops 1207959552 | bytes 5898240 | tf_op jit(solution)/shard_map/dot_general | solution.py:64
  69.8 2.2 %convert_reduce_fusion = (f32[384,64]{0,1:T(8,128)S(1)}, bf16[384,1024]{0,1:T(8,128)(2,1)S(1)}) fusion(f32[384]{0:T(512)S(1)} %copy-done.2, f32[1024,384]{1,0:T(8,128)S(1)} %fusion.3, f32[1024,384]{1,0:T(8,128)S(1)} %fusion.5, f32[1024,384]{1,0:T(8,128)S(1)} %fusion.7, f32[1024,384]{1,0:T(8,128)S(1)} %fusion.9, bf16[5,384,1536]{2,1,0:T(8,128)(2,1)S(1)} %bitcast.36, ...), kind=kOutput, calls=%fused_computation.30 | convolution fusion | flops 1211867136 | bytes 12290048 | tf_op jit(solution)/shard_map/dot_general | solution.py:64
  72.1 0.1 multiply_reduce_fusion
  72.2 0.9 %fusion.41 = f32[64,64]{0,1:T(8,128)S(1)} fusion(bf16[64,1536]{1,0:T(8,128)(2,1)} %param.12, s32[]{:T(128)S(6)} %select_n.28, f32[384,64]{0,1:T(8,128)S(1)} %get-tuple-element.18), kind=kOutput, calls=%fused_computation.48 | convolution fusion | flops 3194880 | bytes 163844 | tf_op jit(solution)/shard_map/dot_general | solution.py:78
  73.1 15.2 %all-reduce = (f32[64,64]{0,1:T(8,128)S(1)}, f32[64]{0:T(128)S(1)}) all-reduce(f32[64,64]{0,1:T(8,128)S(1)} %fusion.41, f32[64]{0:T(128)S(1)} %multiply_reduce_fusion), channel_id=1, replica_groups=mesh['row'=8,'col'=4] {'col'}, use_global_device_ids=true, to_apply=%region_3.4 | all-reduce | flops 4160 | bytes 33280 | tf_op jit(solution)/shard_map/psum | solution.py:81
  88.4 0.1 collective-permute-start.2
  88.5 1.2 %copy.42 = bf16[384,1024]{1,0:T(8,128)(2,1)} copy(bf16[384,1024]{0,1:T(8,128)(2,1)S(1)} %get-tuple-element.19) | data formatting | bytes 1572864
  89.7 0.2 copy.40
  89.9 0.1 fusion.44
  90.0 0.1 copy.41
  90.1 0.2 mul.102
  90.4 0.3 copy-done.1
  90.7 2.1 %fusion.29 = bf16[64,32,128]{2,1,0:T(8,128)(2,1)} fusion(f32[32,1024]{1,0:T(8,128)S(1)} %mul.102, f32[64,1024]{1,0:T(8,128)S(1)} %copy.40, bf16[64,32,128]{2,1,0:T(8,128)(2,1)S(1)} %copy-done.1, f32[128]{0:T(128)S(1)} %copy-done.3, bf16[1024,128]{1,0:T(8,128)(2,1)S(1)} %copy-done), kind=kOutput, calls=%fused_computation.33 | convolution fusion | flops 542113792 | bytes 1704448 | tf_op jit(solution)/shard_map/dot_general | solution.py:101
  (17 shorter events, 0.1 us)
Async XLA Ops:
  0.6 89.7 %copy-start = (bf16[1024,128]{1,0:T(8,128)(2,1)S(1)}, bf16[1024,128]{1,0:T(8,128)(2,1)}, u32[]{:S(2)}) copy-start(bf16[1024,128]{1,0:T(8,128)(2,1)} %param.14) | copy-start | bytes 786436
  15.3 2.6 %collective-permute-start = (bf16[384,16]{0,1:T(8,128)(2,1)S(1)}, bf16[384,16]{0,1:T(8,128)(2,1)S(1)}, u32[]{:S(2)}, u32[]{:S(2)}) collective-permute-start(bf16[384,16]{0,1:T(8,128)(2,1)S(1)} %get-tuple-element.14), channel_id=1, source_target_pairs={{0,4},{4,8},{8,12},{12,16},{16,20},{20,24},{24,28},{1,5},{5,9},{9,... | collective-permute-start | bytes 36872 | tf_op jit(solution)/shard_map/ppermute | solution.py:22
  16.6 4.9 %collective-permute-start.1 = (bf16[384,16]{0,1:T(8,128)(2,1)S(1)}, bf16[384,16]{0,1:T(8,128)(2,1)S(1)}, u32[]{:S(2)}, u32[]{:S(2)}) collective-permute-start(bf16[384,16]{0,1:T(8,128)(2,1)S(1)} %get-tuple-element.15), channel_id=1, source_target_pairs={{4,0},{8,4},{12,8},{16,12},{20,16},{24,20},{28,24},{5,1},{9,5},{13... | collective-permute-start | bytes 36872 | tf_op jit(solution)/shard_map/ppermute | solution.py:24
  21.6 41.0 %slice-start = ((s8[5898240]{0:T(1024)(128)(4,1)}), s8[4194304]{0:T(1024)(128)(4,1)S(1)}, s32[]{:S(2)}) async-start(s8[5898240]{0:T(1024)(128)(4,1)} %bitcast.35), calls=%async_computation.1 | async-start | bytes 8388608
  21.9 40.7 %slice-start.1 = ((s8[5898240]{0:T(1024)(128)(4,1)}), s8[1703936]{0:T(1024)(128)(4,1)S(1)}, s32[]{:S(2)}) async-start(s8[5898240]{0:T(1024)(128)(4,1)} %bitcast.35), calls=%async_computation.2 | async-start | bytes 3407872
  68.0 1.8 %copy-start.2 = (f32[384]{0:T(512)S(1)}, f32[384]{0:T(512)}, u32[]{:S(2)}) copy-start(f32[384]{0:T(512)} %param.10) | copy-start | bytes 4612
  88.4 1.5 %collective-permute-start.2 = (bf16[64,32]{0,1:T(8,128)(2,1)S(1)}, bf16[64,32]{0,1:T(8,128)(2,1)S(1)}, u32[]{:S(2)}, u32[]{:S(2)}) collective-permute-start(bf16[64,32]{0,1:T(8,128)(2,1)S(1)} %get-tuple-element.17), channel_id=1, source_target_pairs={{0,4},{4,0},{8,12},{12,8},{16,20},{20,16},{24,28},{28,24},{1,5},{5... | collective-permute-start | bytes 12296 | tf_op jit(solution)/shard_map/ppermute | solution.py:38
  89.7 1.0 %copy-start.1 = (bf16[64,32,128]{2,1,0:T(8,128)(2,1)S(1)}, bf16[64,32,128]{2,1,0:T(8,128)(2,1)}, u32[]{:S(2)}) copy-start(bf16[64,32,128]{2,1,0:T(8,128)(2,1)} %param.13) | copy-start | bytes 1572868
  89.7 1.0 %copy-start.3 = (f32[128]{0:T(128)S(1)}, f32[128]{0:T(128)}, u32[]{:S(2)}) copy-start(f32[128]{0:T(128)} %param.15) | copy-start | bytes 1540
